TPU v7x, 256 devices: a whole 4x4x8 slice. The times are simulated.
256 devices in a mesh: row: 8 (over x, core), col: 32 (over z, y).
Axes of the slice: x: 4, y: 4, z: 8, core: 2. Of those that a mesh axis runs over, the one named last changes fastest.
Arguments:
- leaf_rhs: bfloat16 [6144, 128, 512], P(('row', 'col')), may hold values from -6 to 6
- leaf_inverse: bfloat16 [6144, 128, 128], P(('row', 'col')), as said below
- leaf_link: bfloat16 [6144, 128, 128], P(('row', 'col')), may hold values from -0.109375 to 0.109375
- leaf_parent: int32 [6144], P(('row', 'col')), may hold values from 0 to 255, as said below
- node_rhs: bfloat16 [256, 128, 512], P(('row', 'col')), may hold values from -6 to 6
- node_inverse: bfloat16 [256, 128, 128], P(('row', 'col')), as said below
- node_link: bfloat16 [256, 128, 128], P(('row', 'col')), may hold values from -0.25 to 0.25
- node_parent: int32 [256], P('row'), may hold values from 0 to 63, as said below
- middle_rhs: bfloat16 [64, 128, 512], P('row'), may hold values from -6 to 6
- middle_inverse: bfloat16 [64, 128, 128], P('row'), as said below
- middle_link: bfloat16 [64, 128, 128], P('row'), may hold values from -0.125 to 0.125
- middle_parent: int32 [64], P('row'), may hold values from 0 to 3
- top_rhs: bfloat16 [4, 128, 512], replicated, may hold values from -6 to 6
- top_inverse: bfloat16 [4, 128, 128], replicated, as said below
Outputs:
- leaf_result: bfloat16 [6144, 128, 512], P(('row', 'col'))
- node_result: bfloat16 [256, 128, 512], P(('row', 'col'))
- middle_result: bfloat16 [64, 128, 512], P('row')
- top_result: bfloat16 [4, 128, 512], replicated
Inputs may be any that keep to these rules, and one draw needn't show every extreme that they name: `leaf_parent`: the parent of a leaf held by the device at grid row r lies in block row r: it is r * 32 + c for some c below 32. `node_parent`: the parent of second-level supernode r * 32 + c is r * 8 + j for some j below 8. `leaf_inverse`: each block is lower triangular. `node_inverse`: each block is lower triangular. `middle_inverse`: each block is lower triangular. `top_inverse`: each block is lower triangular.
All inputs are finite; a program needn't handle non-finite values.
Results may differ from a plain program's by a relative error of at most 0.017.
Values may be sent and summed in bfloat16 or wider, within the bound.
No kernel may reach another device: no remote copies, remote signals or barrier semaphores. Data moves between devices by JAX's collectives and lax.ppermute only.
A program may use at most 128 MiB of HBM per device.

v0:
```python
import jax
import jax.numpy as jnp
from jax import lax
from jax.sharding import PartitionSpec as P


def apply_block(matrix, vectors):
    return jnp.einsum("nij,njr->nir", matrix, vectors, preferred_element_type=jnp.float32)


def apply_transposed(matrix, vectors):
    return jnp.einsum("nij,nir->njr", matrix, vectors, preferred_element_type=jnp.float32)


def slot_sums(targets, count, values):
    slots = lax.iota(jnp.int32, count)
    select = (slots[:, None] == targets[None, :]).astype(jnp.float32)
    return jnp.einsum("sk,kwr->swr", select, values, precision=lax.Precision.HIGHEST)


def local(
    leaf_rhs,
    leaf_inverse,
    leaf_link,
    leaf_parent,
    node_rhs,
    node_inverse,
    node_link,
    node_parent,
    middle_rhs,
    middle_inverse,
    middle_link,
    middle_parent,
    top_rhs,
    top_inverse,
):
    peers = lax.axis_size("col")
    col_index = lax.axis_index("col")
    middle_count = middle_rhs.shape[0]
    top_count = top_rhs.shape[0]
    leaf_target = leaf_parent % peers
    middle_target = node_parent % middle_count
    leaf_solved = apply_block(leaf_inverse, leaf_rhs).astype(jnp.bfloat16)
    leaf_update = apply_block(leaf_link, leaf_solved)
    node_sum = lax.psum_scatter(
        slot_sums(leaf_target, lax.axis_size("col") * 1, leaf_update),
        "col",
        scatter_dimension=0,
        tiled=True,
    )
    node_y = (node_rhs.astype(jnp.float32) - node_sum).astype(jnp.bfloat16)
    node_solved = apply_block(node_inverse, node_y).astype(jnp.bfloat16)
    own_target = lax.dynamic_slice_in_dim(middle_target, col_index, 1)
    middle_term = slot_sums(own_target, middle_count, apply_block(node_link, node_solved))
    middle_sum = lax.psum(middle_term, "col")
    middle_y = (middle_rhs.astype(jnp.float32) - middle_sum).astype(jnp.bfloat16)
    middle_solved = apply_block(middle_inverse, middle_y).astype(jnp.bfloat16)
    top_term = slot_sums(middle_parent, top_count, apply_block(middle_link, middle_solved))
    top_sum = lax.psum(top_term, "row")
    top_y = (top_rhs.astype(jnp.float32) - top_sum).astype(jnp.bfloat16)
    top_solved = apply_block(top_inverse, top_y).astype(jnp.bfloat16)
    top_result = apply_transposed(top_inverse, top_solved).astype(jnp.bfloat16)
    middle_w = (
        middle_solved.astype(jnp.float32) - apply_transposed(middle_link, top_result[middle_parent])
    ).astype(jnp.bfloat16)
    middle_result = apply_transposed(middle_inverse, middle_w).astype(jnp.bfloat16)
    node_w = (
        node_solved.astype(jnp.float32) - apply_transposed(node_link, middle_result[own_target])
    ).astype(jnp.bfloat16)
    node_result = apply_transposed(node_inverse, node_w).astype(jnp.bfloat16)
    row_result = lax.all_gather(node_result, "col", axis=0, tiled=True)
    leaf_w = (
        leaf_solved.astype(jnp.float32) - apply_transposed(leaf_link, row_result[leaf_target])
    ).astype(jnp.bfloat16)
    leaf_result = apply_transposed(leaf_inverse, leaf_w).astype(jnp.bfloat16)
    return (leaf_result, node_result, middle_result, top_result)


def solution(mesh):
    placed = (
        P(("row", "col"), None, None),
        P(("row", "col"), None, None),
        P(("row", "col"), None, None),
        P(("row", "col")),
        P(("row", "col"), None, None),
        P(("row", "col"), None, None),
        P(("row", "col"), None, None),
        P("row"),
        P("row", None, None),
        P("row", None, None),
        P("row", None, None),
        P("row"),
        P(),
        P(),
    )
    return jax.shard_map(
        local,
        mesh=mesh,
        in_specs=placed,
        out_specs=(
            P(("row", "col"), None, None),
            P(("row", "col"), None, None),
            P("row", None, None),
            P(),
        ),
        check_vma=False,
    )
```

profile of v0, /device:TPU:16, one launch (start us, length us, event | category | flops | bytes accessed | tf_op | source)
XLA Modules:
  0.0 620.0 jit_solution(1758936488983695656)
XLA Ops:
  7.2 1.8 copy-done
  9.1 2.2 convolution_convert_fusion
  11.3 1.7 copy-done.2
  12.9 3.7 convolution_bitcast_fusion
  16.6 6.7 %copy.50 = f32[24,128,512]{2,0,1:T(8,128)} copy(f32[24,128,512]{1,2,0:T(8,128)} %convolution_bitcast_fusion) | data formatting | bytes 12582912 | tf_op jit(solution)/shard_map/nij,njr->nir/dot_general | solution.py:8
  23.3 7.5 %fusion.22 = f32[32,128,512]{2,0,1:T(8,128)S(1)} fusion(f32[24,128,512]{2,0,1:T(8,128)} %copy.50, s32[24]{0:T(128)S(1)} %get-tuple-element.32), kind=kOutput, calls=%fused_computation.35 | convolution fusion | flops 603980544 | bytes 14680160 | tf_op jit(solution)/shard_map/sk,kwr->swr/dot_general | solution.py:18
  30.9 8.1 %copy.51 = f32[32,128,512]{2,1,0:T(8,128)} copy(f32[32,128,512]{2,0,1:T(8,128)S(1)} %fusion.22) | data formatting | bytes 16777216 | tf_op jit(solution)/shard_map/sk,kwr->swr/dot_general | solution.py:18
  40.9 229.2 %reduce-scatter.2.cloned.1.call-done = f32[1,128,512]{2,1,0:T(8,128)} async-done(((f32[32,128,512]{2,1,0:T(8,128)}), f32[1,128,512]{2,1,0:T(8,128)}) %reduce-scatter.2.cloned.1.call-update) | async-done | bytes 262160 | tf_op jit(solution)/shard_map/reduce_scatter | solution.py:45
  271.6 1.6 broadcast_multiply_fusion
  273.5 152.5 %all-reduce.3.cloned.1.call-done = f32[8,128,512]{2,1,0:T(8,128)} async-done(((f32[8,128,512]{2,1,0:T(8,128)}), f32[8,128,512]{2,1,0:T(8,128)}) %all-reduce.3.cloned.1.call-update) | async-done | bytes 2097168 | tf_op jit(solution)/shard_map/psum | solution.py:55
  426.0 2.1 convolution_convert_fusion.2
  428.1 1.8 convolution_bitcast_fusion.1
  429.9 2.2 copy.54
  436.6 64.0 %all-reduce.5.cloned.1.call-done = f32[4,128,512]{2,1,0:T(8,128)} async-done(((f32[4,128,512]{2,1,0:T(8,128)}), f32[4,128,512]{2,1,0:T(8,128)}) %all-reduce.5.cloned.1.call-update) | async-done | bytes 1048592 | tf_op jit(solution)/shard_map/psum | solution.py:59
  500.7 1.7 fusion.7
  502.4 1.7 gather_fusion
  504.1 1.9 convolution_convert_fusion.1
  508.1 1.7 copy.62
  509.7 1.3 copy.63
  511.0 79.7 %all-gather.3.cloned.1.call-done = bf16[4096,512]{0,1:T(8,128)(2,1)} async-done(((bf16[128,512]{0,1:T(8,128)(2,1)}), bf16[4096,512]{0,1:T(8,128)(2,1)}) %all-gather.3.cloned.1.call-update) | async-done | bytes 4194320 | tf_op jit(solution)/shard_map/all_gather | solution.py:71
  590.7 6.5 %copy.71 = bf16[4096,512]{1,0:T(8,128)(2,1)} copy(bf16[4096,512]{0,1:T(8,128)(2,1)} %all-gather.3.cloned.1.call-done) | data formatting | bytes 8388608 | tf_op jit(solution)/shard_map/all_gather | solution.py:71
  597.2 4.7 gather_fusion.1
  601.9 6.9 %convert_bitcast_fusion = bf16[24,128,512]{1,2,0:T(8,128)(2,1)} fusion(bf16[24,128,128]{2,1,0:T(8,128)(2,1)} %param.15, bf16[24,128,512]{2,1,0:T(8,128)(2,1)} %copy-done.2, bf16[24,128,512]{2,1,0:T(8,128)(2,1)} %gather_fusion.1, bf16[24,128,128]{2,1,0:T(8,128)(2,1)} %param.16), kind=kOutput, calls=%fused_computation.5 | convolution fusion | flops 811597824 | bytes 11010048 | tf_op jit(solution)/shard_map/nij,nir->njr/dot_general | solution.py:12
  608.8 4.6 copy.61
  (56 shorter events, 8.2 us)
Async XLA Ops:
  7.2 1.9 copy-start
  7.2 262.9 %reduce-scatter.2.cloned.1.call-start = ((), (), s32[]{:S(2)}) async-start(), calls=%async_computation.1 | async-start | bytes 8650752 | tf_op jit(solution)/shard_map/reduce_scatter | solution.py:45
  9.1 3.8 copy-start.3
  11.2 1.7 copy-start.2
  16.6 6.7 %copy-start.16 = (s32[24]{0:T(128)S(1)}, s32[24]{0:T(128)}, u32[]{:S(2)}) copy-start(s32[24]{0:T(128)} %param.17) | copy-start | bytes 292
  39.0 0.7 copy-start.17
  39.0 231.1 %copy-start.10 = (bf16[1,128,512]{2,1,0:T(8,128)(2,1)S(1)}, bf16[1,128,512]{2,1,0:T(8,128)(2,1)}, u32[]{:S(2)}) copy-start(bf16[1,128,512]{2,1,0:T(8,128)(2,1)} %param.18) | copy-start | bytes 393220
  39.0 231.1 %copy-start.11 = (bf16[1,128,128]{2,1,0:T(8,128)(2,1)S(1)}, bf16[1,128,128]{2,1,0:T(8,128)(2,1)}, u32[]{:S(2)}) copy-start(bf16[1,128,128]{2,1,0:T(8,128)(2,1)} %param.19) | copy-start | bytes 98308
  39.0 232.3 %copy-start.13 = (bf16[1,128,128]{2,1,0:T(8,128)(2,1)S(1)}, bf16[1,128,128]{2,1,0:T(8,128)(2,1)}, u32[]{:S(2)}) copy-start(bf16[1,128,128]{2,1,0:T(8,128)(2,1)} %param.20) | copy-start | bytes 98308
  39.0 387.0 %copy-start.4 = (bf16[8,128,128]{2,1,0:T(8,128)(2,1)S(1)}, bf16[8,128,128]{2,1,0:T(8,128)(2,1)}, u32[]{:S(2)}) copy-start(bf16[8,128,128]{2,1,0:T(8,128)(2,1)} %param.23) | copy-start | bytes 786436
  39.0 387.0 %copy-start.5 = (bf16[8,128,512]{2,1,0:T(8,128)(2,1)S(1)}, bf16[8,128,512]{2,1,0:T(8,128)(2,1)}, u32[]{:S(2)}) copy-start(bf16[8,128,512]{2,1,0:T(8,128)(2,1)} %param.22) | copy-start | bytes 3145732
  39.0 387.0 %all-reduce.3.cloned.1.call-start = ((), (), s32[]{:S(2)}) async-start(), calls=%async_computation.2 | async-start | bytes 4194304 | tf_op jit(solution)/shard_map/psum | solution.py:55
  273.3 154.9 %copy-start.6 = (bf16[8,128,128]{2,1,0:T(8,128)(2,1)S(1)}, bf16[8,128,128]{2,1,0:T(8,128)(2,1)}, u32[]{:S(2)}) copy-start(bf16[8,128,128]{2,1,0:T(8,128)(2,1)} %param.24) | copy-start | bytes 786436
  273.3 227.4 %all-reduce.5.cloned.1.call-start = ((), (), s32[]{:S(2)}) async-start(), calls=%async_computation.3 | async-start | bytes 2097152 | tf_op jit(solution)/shard_map/psum | solution.py:59
  428.1 4.0 copy-start.15
  433.3 67.4 %copy-start.8 = (bf16[4,128,128]{2,1,0:T(8,128)(2,1)S(1)}, bf16[4,128,128]{2,1,0:T(8,128)(2,1)}, u32[]{:S(2)}) copy-start(bf16[4,128,128]{2,1,0:T(8,128)(2,1)} %param.27) | copy-start | bytes 393220
  433.3 67.4 %copy-start.9 = (bf16[4,128,512]{2,1,0:T(8,128)(2,1)S(1)}, bf16[4,128,512]{2,1,0:T(8,128)(2,1)}, u32[]{:S(2)}) copy-start(bf16[4,128,512]{2,1,0:T(8,128)(2,1)} %param.26) | copy-start | bytes 1572868
  434.6 69.5 %copy-start.7 = (bf16[8,128,128]{2,1,0:T(8,128)(2,1)S(1)}, bf16[8,128,128]{2,1,0:T(8,128)(2,1)}, u32[]{:S(2)}) copy-start(bf16[8,128,128]{2,1,0:T(8,128)(2,1)} %param.24) | copy-start | bytes 786436
  434.6 156.1 %all-gather.3.cloned.1.call-start = ((), (), s32[]{:S(2)}) async-start(), calls=%async_computation.4 | async-start | bytes 4325376 | tf_op jit(solution)/shard_map/all_gather | solution.py:71
  502.4 3.6 copy-start.12
  502.4 3.6 copy-start.14
  601.9 11.5 %copy-start.1 = (bf16[24,128,512]{2,1,0:T(8,128)(2,1)S(1)}, bf16[24,128,512]{2,1,0:T(8,128)(2,1)}, u32[]{:S(2)}) copy-start(bf16[24,128,512]{2,1,0:T(8,128)(2,1)} %param.14) | copy-start | bytes 9437188
Sparse Core Ops, SparseCore 0:
  39.1 230.9 reduce-scatter.1
  274.0 151.9 all-reduce.2
  434.7 65.9 all-reduce.4
  507.2 83.5 all-gather.2
where the time goes:
time: 621 us; the launch traced here: 620 us
  waiting for transfers between devices  525 us (85%)
  local copies, waits for them, and re-layouts  44.6 us (7%)
  matrix products  31.2 us (5%)
  between operations  16 us (3%)
    reduce_scatter x1, waiting for transfers between devices, local(): lax.psum_scatter(slot_sums(leaf_target, lax.axis_size('col') * 1, leaf_up...  229 us
    psum x1, waiting for transfers between devices, local(): middle_sum = lax.psum(middle_term, 'col')  152 us
    all_gather x1, waiting for transfers between devices, local(): row_result = lax.all_gather(node_result, 'col', axis=0, tiled=True)  79.7 us
    psum x1, waiting for transfers between devices, local(): top_sum = lax.psum(top_term, 'row')  64 us
    unnamed x40, local copies, waits for them, and re-layouts  12.7 us
  transfers between devices with their start and end apart: 4, of which 4 were waited for; matrix products, arithmetic and copies ran while one was open for 1% of the time, Pallas kernels for 0%

commit v1 on v0

--- a/solution.py
+++ b/solution.py
@@ -2,6 +2,13 @@
 import jax.numpy as jnp
 from jax import lax
 from jax.sharding import PartitionSpec as P
+
+
+def build_ways_now(xx, chip_axis):
+    seen_now = lax.all_to_all(
+        jnp.stack([xx for _ in range(lax.psum(1, chip_axis))], axis=0), chip_axis, 0, 0
+    )
+    return jnp.concatenate(seen_now, axis=0)
 
 
 def apply_block(matrix, vectors):
@@ -68,7 +75,7 @@
         node_solved.astype(jnp.float32) - apply_transposed(node_link, middle_result[own_target])
     ).astype(jnp.bfloat16)
     node_result = apply_transposed(node_inverse, node_w).astype(jnp.bfloat16)
-    row_result = lax.all_gather(node_result, "col", axis=0, tiled=True)
+    row_result = build_ways_now(node_result, "col")
     leaf_w = (
         leaf_solved.astype(jnp.float32) - apply_transposed(leaf_link, row_result[leaf_target])
     ).astype(jnp.bfloat16)

time: 621 us -> 641 us (1.032)
  starting transfers between devices: 0.34 us -> 10.5 us
  waiting for transfers between devices: 525 us -> 535 us
    all_to_all x0 -> x1, waiting for transfers between devices: none -> 89.4 us  [build_ways_now(): lax.all_to_all(jnp.stack([xx for _ in range(lax.psum(1, chip_axis))], axi...]
    all_gather x1 -> x0, waiting for transfers between devices: 79.7 us -> none  [local(): row_result = lax.all_gather(node_result, 'col', axis=0, tiled=True)]
    all_to_all x0 -> x1, starting transfers between devices: none -> 10.2 us  [build_ways_now(): lax.all_to_all(jnp.stack([xx for _ in range(lax.psum(1, chip_axis))], axi...]
    all_gather x1 -> x0, local copies, waits for them, and re-layouts: 6.5 us -> none  [local(): row_result = lax.all_gather(node_result, 'col', axis=0, tiled=True)]
where the time goes in v1:
time: 641 us; the launch traced here: 635 us
  waiting for transfers between devices  535 us (83%)
  local copies, waits for them, and re-layouts  39.8 us (6%)
  matrix products  30.6 us (5%)
  between operations  16 us (2%)
  starting transfers between devices  10.5 us (2%)
    reduce_scatter x1, waiting for transfers between devices, local(): lax.psum_scatter(slot_sums(leaf_target, lax.axis_size('col') * 1, leaf_up...  229 us
    psum x1, waiting for transfers between devices, local(): middle_sum = lax.psum(middle_term, 'col')  153 us
    all_to_all x1, waiting for transfers between devices, build_ways_now(): lax.all_to_all(jnp.stack([xx for _ in range(lax.psum(1, chip_axis))], axi...  89.4 us
    psum x1, waiting for transfers between devices, local(): top_sum = lax.psum(top_term, 'row')  64.1 us
  transfers between devices with their start and end apart: 4, of which 4 were waited for; matrix products, arithmetic and copies ran while one was open for 1% of the time, Pallas kernels for 0%

profile of v1, /device:TPU:16, one launch (start us, length us, event | category | flops | bytes accessed | tf_op | source)
XLA Modules:
  0.0 634.6 jit_solution(12836518238427122908)
XLA Ops:
  7.2 1.8 copy-done
  9.1 2.2 convolution_convert_fusion
  11.3 1.7 copy-done.2
  12.9 3.7 convolution_bitcast_fusion
  16.6 6.7 %copy.82 = f32[24,128,512]{2,0,1:T(8,128)} copy(f32[24,128,512]{1,2,0:T(8,128)} %convolution_bitcast_fusion) | data formatting | bytes 12582912 | tf_op jit(solution)/shard_map/nij,njr->nir/dot_general | solution.py:15
  23.3 7.5 %fusion.22 = f32[32,128,512]{2,0,1:T(8,128)S(1)} fusion(f32[24,128,512]{2,0,1:T(8,128)} %copy.82, s32[24]{0:T(128)S(1)} %get-tuple-element.40), kind=kOutput, calls=%fused_computation.35 | convolution fusion | flops 603980544 | bytes 14680160 | tf_op jit(solution)/shard_map/sk,kwr->swr/dot_general | solution.py:25
  30.9 8.1 %copy.83 = f32[32,128,512]{2,1,0:T(8,128)} copy(f32[32,128,512]{2,0,1:T(8,128)S(1)} %fusion.22) | data formatting | bytes 16777216 | tf_op jit(solution)/shard_map/sk,kwr->swr/dot_general | solution.py:25
  40.9 229.4 %reduce-scatter.2.cloned.1.call-done = f32[1,128,512]{2,1,0:T(8,128)} async-done(((f32[32,128,512]{2,1,0:T(8,128)}), f32[1,128,512]{2,1,0:T(8,128)}) %reduce-scatter.2.cloned.1.call-update) | async-done | bytes 262160 | tf_op jit(solution)/shard_map/reduce_scatter | solution.py:52
  271.8 1.6 broadcast_multiply_fusion
  273.7 152.5 %all-reduce.3.cloned.1.call-done = f32[8,128,512]{2,1,0:T(8,128)} async-done(((f32[8,128,512]{2,1,0:T(8,128)}), f32[8,128,512]{2,1,0:T(8,128)}) %all-reduce.3.cloned.1.call-update) | async-done | bytes 2097168 | tf_op jit(solution)/shard_map/psum | solution.py:62
  426.2 2.1 convolution_convert_fusion.2
  428.3 1.8 convolution_bitcast_fusion.1
  430.1 2.2 copy.86
  436.8 64.1 %all-reduce.5.cloned.1.call-done = f32[4,128,512]{2,1,0:T(8,128)} async-done(((f32[4,128,512]{2,1,0:T(8,128)}), f32[4,128,512]{2,1,0:T(8,128)}) %all-reduce.5.cloned.1.call-update) | async-done | bytes 1048592 | tf_op jit(solution)/shard_map/psum | solution.py:66
  500.9 1.7 fusion.7
  502.6 1.7 gather_fusion
  504.3 1.9 convolution_convert_fusion.1
  506.7 2.5 stack.2
  509.1 10.2 %all-to-all-start = ((bf16[32,1,128,512]{3,2,1,0:T(8,128)(2,1)}), bf16[32,1,128,512]{3,2,1,0:T(8,128)(2,1)}, u32[]{:S(2)}, u32[]{:S(2)}) async-start(bf16[32,1,128,512]{3,2,1,0:T(8,128)(2,1)} %stack.2), calls=%async_computation.1 | async-start | bytes 8388608 | tf_op jit(solution)/shard_map/all_to_all | solution.py:8
  521.1 1.3 copy.95
  522.4 89.4 %all-to-all-done = bf16[32,1,128,512]{3,2,1,0:T(8,128)(2,1)} async-done(((bf16[32,1,128,512]{3,2,1,0:T(8,128)(2,1)}), bf16[32,1,128,512]{3,2,1,0:T(8,128)(2,1)}, u32[]{:S(2)}, u32[]{:S(2)}) %all-to-all-start) | async-done | bytes 4194336 | tf_op jit(solution)/shard_map/all_to_all | solution.py:8
  611.8 4.7 gather_fusion.1
  616.6 6.9 %convert_bitcast_fusion = bf16[24,128,512]{1,2,0:T(8,128)(2,1)} fusion(bf16[24,128,128]{2,1,0:T(8,128)(2,1)} %param.15, bf16[24,128,512]{2,1,0:T(8,128)(2,1)} %copy-done.2, bf16[24,128,512]{2,1,0:T(8,128)(2,1)} %gather_fusion.1, bf16[24,128,128]{2,1,0:T(8,128)(2,1)} %param.16), kind=kOutput, calls=%fused_computation.5 | convolution fusion | flops 811597824 | bytes 11010048 | tf_op jit(solution)/shard_map/nij,nir->njr/dot_general | solution.py:19
  623.5 4.6 copy.93
  (56 shorter events, 8.3 us)
Async XLA Ops:
  7.2 1.9 copy-start
  7.2 263.1 %reduce-scatter.2.cloned.1.call-start = ((), (), s32[]{:S(2)}) async-start(), calls=%async_computation.2 | async-start | bytes 8650752 | tf_op jit(solution)/shard_map/reduce_scatter | solution.py:52
  9.1 3.8 copy-start.3
  11.2 1.7 copy-start.2
  16.6 6.7 %copy-start.16 = (s32[24]{0:T(128)S(1)}, s32[24]{0:T(128)}, u32[]{:S(2)}) copy-start(s32[24]{0:T(128)} %param.17) | copy-start | bytes 292
  39.0 0.7 copy-start.17
  39.0 231.3 %copy-start.10 = (bf16[1,128,512]{2,1,0:T(8,128)(2,1)S(1)}, bf16[1,128,512]{2,1,0:T(8,128)(2,1)}, u32[]{:S(2)}) copy-start(bf16[1,128,512]{2,1,0:T(8,128)(2,1)} %param.18) | copy-start | bytes 393220
  39.0 231.3 %copy-start.11 = (bf16[1,128,128]{2,1,0:T(8,128)(2,1)S(1)}, bf16[1,128,128]{2,1,0:T(8,128)(2,1)}, u32[]{:S(2)}) copy-start(bf16[1,128,128]{2,1,0:T(8,128)(2,1)} %param.19) | copy-start | bytes 98308
  39.0 232.5 %copy-start.13 = (bf16[1,128,128]{2,1,0:T(8,128)(2,1)S(1)}, bf16[1,128,128]{2,1,0:T(8,128)(2,1)}, u32[]{:S(2)}) copy-start(bf16[1,128,128]{2,1,0:T(8,128)(2,1)} %param.20) | copy-start | bytes 98308
  39.0 387.2 %copy-start.4 = (bf16[8,128,128]{2,1,0:T(8,128)(2,1)S(1)}, bf16[8,128,128]{2,1,0:T(8,128)(2,1)}, u32[]{:S(2)}) copy-start(bf16[8,128,128]{2,1,0:T(8,128)(2,1)} %param.23) | copy-start | bytes 786436
  39.0 387.2 %copy-start.5 = (bf16[8,128,512]{2,1,0:T(8,128)(2,1)S(1)}, bf16[8,128,512]{2,1,0:T(8,128)(2,1)}, u32[]{:S(2)}) copy-start(bf16[8,128,512]{2,1,0:T(8,128)(2,1)} %param.22) | copy-start | bytes 3145732
  39.0 387.2 %all-reduce.3.cloned.1.call-start = ((), (), s32[]{:S(2)}) async-start(), calls=%async_computation.3 | async-start | bytes 4194304 | tf_op jit(solution)/shard_map/psum | solution.py:62
  273.4 154.9 %copy-start.6 = (bf16[8,128,128]{2,1,0:T(8,128)(2,1)S(1)}, bf16[8,128,128]{2,1,0:T(8,128)(2,1)}, u32[]{:S(2)}) copy-start(bf16[8,128,128]{2,1,0:T(8,128)(2,1)} %param.24) | copy-start | bytes 786436
  273.5 227.4 %all-reduce.5.cloned.1.call-start = ((), (), s32[]{:S(2)}) async-start(), calls=%async_computation.4 | async-start | bytes 2097152 | tf_op jit(solution)/shard_map/psum | solution.py:66
  428.3 4.0 copy-start.15
  433.5 67.4 %copy-start.8 = (bf16[4,128,128]{2,1,0:T(8,128)(2,1)S(1)}, bf16[4,128,128]{2,1,0:T(8,128)(2,1)}, u32[]{:S(2)}) copy-start(bf16[4,128,128]{2,1,0:T(8,128)(2,1)} %param.27) | copy-start | bytes 393220
  433.5 67.4 %copy-start.9 = (bf16[4,128,512]{2,1,0:T(8,128)(2,1)S(1)}, bf16[4,128,512]{2,1,0:T(8,128)(2,1)}, u32[]{:S(2)}) copy-start(bf16[4,128,512]{2,1,0:T(8,128)(2,1)} %param.26) | copy-start | bytes 1572868
  434.8 69.5 %copy-start.7 = (bf16[8,128,128]{2,1,0:T(8,128)(2,1)S(1)}, bf16[8,128,128]{2,1,0:T(8,128)(2,1)}, u32[]{:S(2)}) copy-start(bf16[8,128,128]{2,1,0:T(8,128)(2,1)} %param.24) | copy-start | bytes 786436
  502.6 3.6 copy-start.12
  502.6 3.6 copy-start.14
  509.1 102.7 %all-to-all-start = ((bf16[32,1,128,512]{3,2,1,0:T(8,128)(2,1)}), bf16[32,1,128,512]{3,2,1,0:T(8,128)(2,1)}, u32[]{:S(2)}, u32[]{:S(2)}) async-start(bf16[32,1,128,512]{3,2,1,0:T(8,128)(2,1)} %stack.2), calls=%async_computation.1 | async-start | bytes 8388608 | tf_op jit(solution)/shard_map/all_to_all | solution.py:8
  616.6 11.5 %copy-start.1 = (bf16[24,128,512]{2,1,0:T(8,128)(2,1)S(1)}, bf16[24,128,512]{2,1,0:T(8,128)(2,1)}, u32[]{:S(2)}) copy-start(bf16[24,128,512]{2,1,0:T(8,128)(2,1)} %param.14) | copy-start | bytes 9437188
Sparse Core Ops, SparseCore 0:
  39.1 231.0 reduce-scatter.1
  274.2 151.9 all-reduce.2
  434.9 65.9 all-reduce.4
